TPU v7x, 256 devices: a whole 4x4x8 slice. The times are simulated.
256 devices in a mesh: dp: 8 (over x, core), expert: 16 (over y, z_hi), tensor: 2 (over z_lo).
Axes of the slice: x: 4, y: 4, z: 8 (z_hi: 4, z_lo: 2; z = z_hi * 2 + z_lo), core: 2. Of those that a mesh axis runs over, the one named last changes fastest.
Arguments:
- tokens: bfloat16 [1024, 7168], P(('dp', 'expert'), 'tensor'), may hold values from -6 to 6
- upstream: bfloat16 [1024, 7168], P(('dp', 'expert'), 'tensor'), may hold values from -3 to 3
- probs: bfloat16 [1024, 8], P(('dp', 'expert')), may hold values from 0.049804688 to 0.59765625
- routing: int32 [1024, 8], P(('dp', 'expert')), may hold values from 0 to 15, all different within a row; in each aligned block of 8 rows (0 to 7, 8 to 15, ...) at most 5 rows name the same one
- row_rollout: int32 [1024], P(('dp', 'expert')), may hold values from 0 to 255
- group_ids: int32 [256], replicated, may hold values from 0 to 31
- rewards: int32 [256], replicated, may hold values from 0 to 1
- w_gate: bfloat16 [16, 7168, 2048], P('expert', None, ('dp', 'tensor')), may hold values from -0.0625 to 0.0625
- w_up: bfloat16 [16, 7168, 2048], P('expert', None, ('dp', 'tensor')), may hold values from -0.0625 to 0.0625
- w_down: bfloat16 [16, 2048, 7168], P('expert', ('dp', 'tensor')), may hold values from -0.125 to 0.125
Outputs:
- input_grad: bfloat16 [1024, 7168], P(('dp', 'expert'), 'tensor')
- route_grad: bfloat16 [1024, 8], P(('dp', 'expert'))
- grad_gate: bfloat16 [16, 7168, 2048], P('expert', None, ('dp', 'tensor'))
- grad_up: bfloat16 [16, 7168, 2048], P('expert', None, ('dp', 'tensor'))
- grad_down: bfloat16 [16, 2048, 7168], P('expert', ('dp', 'tensor'))
Inputs may be any that keep to these rules, and one draw needn't show every extreme that they name: `routing`: each row names 8 different experts. Within each aligned block of 8 rows (the tokens of one index pair of dp and expert) no expert is named by more than 5 rows, a bound that some block reaches.
All inputs are finite; a program needn't handle non-finite values.
Results may differ from a plain program's by a relative error of at most 0.025.
Values may be sent and summed in bfloat16 or wider, within the bound.
No kernel may reach another device: no remote copies, remote signals or barrier semaphores. Data moves between devices by JAX's collectives and lax.ppermute only.
A program may use at most 128 MiB of HBM per device.

v0:
```python
import jax
import jax.numpy as jnp
from jax import lax
from jax.sharding import PartitionSpec as P


def advantages(row_rollout, group_ids, rewards):
    same_group = (group_ids[:, None] == group_ids[None, :]).astype(jnp.float32)
    reward_values = rewards.astype(jnp.float32)
    group_total = jnp.dot(same_group, reward_values, precision=lax.Precision.HIGHEST)
    group_count = jnp.sum(same_group, axis=1)
    per_rollout = reward_values - group_total / group_count
    member = (
        row_rollout[:, None] == jnp.arange(per_rollout.shape[0], dtype=jnp.int32)[None, :]
    ).astype(jnp.float32)
    return jnp.dot(member, per_rollout, precision=lax.Precision.HIGHEST)


def selection(routing, probs, experts, capacity):
    route_hits = (
        routing[:, :, None] == jnp.arange(experts, dtype=jnp.int32)[None, None, :]
    ).astype(jnp.float32)
    occupied = jnp.sum(route_hits, axis=1)
    weight = jnp.einsum("rke,rk->re", route_hits, probs.astype(jnp.float32))
    before = jnp.cumsum(occupied, axis=0) - occupied
    slot_index = jnp.arange(capacity, dtype=jnp.float32)
    chosen = occupied.T[:, None, :] * (before.T[:, None, :] == slot_index[None, :, None]).astype(
        jnp.float32
    )
    return (route_hits, weight, chosen)


def shards(tokens, upstream, probs, routing, row_rollout, group_ids, rewards, w_gate, w_up, w_down):
    experts = lax.axis_size("expert")
    dp_size = lax.axis_size("dp")
    tensor_size = lax.axis_size("tensor")
    group_rows, features = tokens.shape
    routes_per_row = routing.shape[1]
    capacity = min(group_rows, 5 * group_rows * routes_per_row // (4 * experts))
    hidden_width = w_gate.shape[2]
    slots = experts * capacity
    advantage = advantages(row_rollout, group_ids, rewards)
    cotangent = (advantage[:, None] * upstream.astype(jnp.float32)).astype(jnp.bfloat16)
    route_hits, weight, chosen = selection(routing, probs, experts, capacity)
    chosen_half = chosen.astype(jnp.bfloat16)
    packed_rows = jnp.einsum(
        "ecr,rf->ecf", chosen_half, tokens, preferred_element_type=jnp.float32
    ).astype(jnp.bfloat16)
    packed_upstream = jnp.einsum(
        "ecr,rf->ecf", chosen_half, cotangent, preferred_element_type=jnp.float32
    ).astype(jnp.bfloat16)
    packed_prob = jnp.einsum("ecr,re->ec", chosen, weight).astype(jnp.bfloat16)
    arrived = (
        lax.all_to_all(packed_rows, "expert", split_axis=0, concat_axis=0, tiled=True),
        lax.all_to_all(packed_upstream, "expert", split_axis=0, concat_axis=0, tiled=True),
        lax.all_to_all(packed_prob, "expert", split_axis=0, concat_axis=0, tiled=True),
    )
    gathered = (
        lax.all_gather(
            arrived[0].reshape(1, slots, features), ("dp", "tensor"), axis=0, tiled=True
        ),
        lax.all_gather(
            arrived[1].reshape(1, slots, features), ("dp", "tensor"), axis=0, tiled=True
        ),
        lax.all_gather(arrived[2].reshape(1, slots), ("dp", "tensor"), axis=0, tiled=True),
    )
    rows_in = gathered[0].reshape(dp_size, tensor_size, experts, capacity, features)
    rows_back = gathered[1].reshape(dp_size, tensor_size, experts, capacity, features)
    slot_prob = gathered[2].reshape(dp_size, tensor_size, experts, capacity)[:, 0]
    layout = "dtecf"
    weights_in = jnp.concatenate([w_gate[0], w_up[0]], axis=1).reshape(
        tensor_size, features, 2 * hidden_width
    )
    weights_out = w_down[0].reshape(hidden_width, tensor_size, features)
    both = jnp.einsum(
        layout + ",tfk->deck", rows_in, weights_in, preferred_element_type=jnp.float32
    )
    gate = both[..., :hidden_width]
    up_part = both[..., hidden_width:]
    back_hidden = jnp.einsum(
        layout + ",htf->dech", rows_back, weights_out, preferred_element_type=jnp.float32
    )
    sigmoid_gate = jax.nn.sigmoid(gate)
    active = gate * sigmoid_gate
    hidden = (active * up_part).astype(jnp.bfloat16)
    hidden_wide = lax.optimization_barrier(hidden).astype(jnp.float32)
    route_part = jnp.sum(hidden_wide * back_hidden, axis=-1)
    scale = slot_prob.astype(jnp.float32)[..., None]
    scaled = scale * back_hidden
    grad_gate_in = scaled * up_part * sigmoid_gate * (1.0 + gate * (1.0 - sigmoid_gate))
    grad_up_in = scaled * active
    grad_inner = jnp.concatenate([grad_gate_in, grad_up_in], axis=-1).astype(jnp.bfloat16)
    weighted = (scale * hidden_wide).astype(jnp.bfloat16)
    grad_down = jnp.einsum(
        "dech," + layout + "->htf", weighted, rows_back, preferred_element_type=jnp.float32
    )
    grad_down = grad_down.reshape(hidden_width, tensor_size * features).astype(jnp.bfloat16)
    grad_both = jnp.einsum(
        layout + ",deck->tfk", rows_in, grad_inner, preferred_element_type=jnp.float32
    )
    grad_both = grad_both.reshape(tensor_size * features, 2 * hidden_width)
    grad_gate = grad_both[:, :hidden_width].astype(jnp.bfloat16)
    grad_up = grad_both[:, hidden_width:].astype(jnp.bfloat16)
    route_total = lax.psum(route_part, ("dp", "tensor"))
    own_route = lax.dynamic_index_in_dim(route_total, lax.axis_index("dp"), 0, keepdims=False)
    first = jnp.int32(0) // slots
    needed = min(
        dp_size,
        (slots * lax.axis_size(("dp", "tensor")) // slots + tensor_size - 1) // tensor_size + 1,
    )
    lead = jnp.clip(first // tensor_size, 0, dp_size - needed)
    part = lax.dynamic_slice_in_dim(grad_inner, lead, needed, 0)
    product = jnp.einsum("deck,tfk->dtecf", part, weights_in, preferred_element_type=jnp.float32)
    product = product.reshape(needed * tensor_size * slots, features)
    own_rows = lax.psum_scatter(
        product.astype(jnp.bfloat16), ("dp", "tensor"), scatter_dimension=0, tiled=True
    ).astype(jnp.float32)
    home = (
        lax.all_to_all(
            own_rows.reshape(experts, capacity, features).astype(jnp.bfloat16),
            "expert",
            split_axis=0,
            concat_axis=0,
            tiled=True,
        ),
        lax.all_to_all(
            own_route.astype(jnp.bfloat16), "expert", split_axis=0, concat_axis=0, tiled=True
        ),
    )
    input_grad = jnp.einsum(
        "ecr,ecf->rf", chosen_half, home[0], preferred_element_type=jnp.float32
    ).astype(jnp.bfloat16)
    per_expert = jnp.einsum("ecr,ec->re", chosen, home[1].astype(jnp.float32))
    route_grad = jnp.einsum("rke,re->rk", route_hits, per_expert).astype(jnp.bfloat16)
    return (input_grad, route_grad, grad_gate[None], grad_up[None], grad_down[None])


def solution(mesh):
    in_specs = (
        P(("dp", "expert"), "tensor"),
        P(("dp", "expert"), "tensor"),
        P(("dp", "expert"), None),
        P(("dp", "expert"), None),
        P(("dp", "expert")),
        P(),
        P(),
        P("expert", None, ("dp", "tensor")),
        P("expert", None, ("dp", "tensor")),
        P("expert", ("dp", "tensor"), None),
    )
    out_specs = (
        P(("dp", "expert"), "tensor"),
        P(("dp", "expert"), None),
        P("expert", None, ("dp", "tensor")),
        P("expert", None, ("dp", "tensor")),
        P("expert", ("dp", "tensor"), None),
    )
    return jax.shard_map(shards, mesh=mesh, in_specs=in_specs, out_specs=out_specs, check_vma=False)
```

profile of v0, /device:TPU:35, one launch (start us, length us, event | category | flops | bytes accessed | tf_op | source)
XLA Modules:
  0.0 505.4 jit_solution(11312434241959555918)
XLA Ops:
  7.2 0.0 copy-start
  7.2 0.0 copy-start.5
  7.2 0.0 all-gather.6.cloned.1.call-start
  7.3 0.9 convert_reduce_fusion
  8.2 0.3 convolution_convert_fusion
  8.6 0.3 copy.58
  8.9 35.1 %all_to_all.33 = bf16[16,5,3584]{2,1,0:T(8,128)(2,1)S(1)} all-to-all(bf16[16,5,3584]{2,1,0:T(8,128)(2,1)S(1)} %copy.58), channel_id=1, replica_groups=mesh['dp'=8,'expert'=16,'tensor'=2] {'expert'}, dimensions={0} | all-to-all | bytes 1146880 | tf_op jit(solution)/shard_map/all_to_all | solution.py:54
  44.0 1.0 reshape.75
  45.1 0.0 all-gather.6.cloned.1.call-update
  45.1 0.0 all-gather.4.cloned.1.call-start
  45.2 0.7 convert_element_type.94
  45.8 0.9 fusion.41
  46.8 1.0 fusion.34
  47.8 0.8 divide_subtract_fusion
  48.5 0.8 convolution_bitcast_fusion.2
  49.4 1.2 convolution_convert_fusion.1
  50.6 0.3 copy.54
  50.9 30.4 %all_to_all.34 = bf16[16,5,3584]{2,1,0:T(8,128)(2,1)S(1)} all-to-all(bf16[16,5,3584]{2,1,0:T(8,128)(2,1)S(1)} %copy.54), channel_id=1, replica_groups=mesh['dp'=8,'expert'=16,'tensor'=2] {'expert'}, dimensions={0} | all-to-all | bytes 1146880 | tf_op jit(solution)/shard_map/all_to_all | solution.py:55
  81.3 1.0 reshape.73
  82.3 0.0 all-gather.4.cloned.1.call-update
  82.4 0.2 fusion.51
  82.6 0.7 copy.52
  83.3 4.2 all-to-all-start
  87.5 0.0 reduce-scatter.2.cloned.1.call-start
  87.5 2.3 reshape_squeeze.3
  89.8 6.4 %all-to-all-done = bf16[16,1,5]{2,1,0:T(2,128)(2,1)S(1)} async-done(((bf16[16,1,5]{2,1,0:T(2,128)(2,1)}), bf16[16,1,5]{2,1,0:T(2,128)(2,1)S(1)}, u32[]{:S(2)}, u32[]{:S(2)}) %all-to-all-start) | async-done | bytes 192 | tf_op jit(solution)/shard_map/all_to_all | solution.py:56
  96.2 0.1 reshape.78
  96.3 29.7 %all-gather = bf16[16,1,80]{2,1,0:T(2,128)(2,1)S(1)} all-gather(bf16[1,1,80]{2,1,0:T(2,128)(2,1)S(1)} %reshape.78), channel_id=1, replica_groups=mesh['dp'=8,'expert'=16,'tensor'=2] {'dp','tensor'}, dimensions={0}, use_global_device_ids=true | all-gather | bytes 2720 | tf_op jit(solution)/shard_map/all_gather | solution.py:65
  126.1 0.1 reshape.72
  126.3 0.1 copy.53
  126.4 0.0 all-gather.6.cloned.1.call-done
  126.4 12.1 %copy.59 = bf16[16,80,3584]{2,0,1:T(8,128)(2,1)} copy(bf16[16,80,3584]{2,1,0:T(8,128)(2,1)} %all-gather.6.cloned.1.call-done) | data formatting | bytes 18350080 | tf_op jit(solution)/shard_map/all_gather | solution.py:59
  138.5 13.8 %reshape.76 = bf16[8,2,16,5,3584]{4,1,0,3,2:T(2,128)(2,1)} reshape(bf16[16,80,3584]{2,0,1:T(8,128)(2,1)} %copy.59) | data formatting | bytes 18350080 | tf_op jit(solution)/shard_map/reshape | solution.py:67
  152.3 35.1 %all-gather.4.cloned.1.call-done = bf16[16,80,3584]{2,1,0:T(8,128)(2,1)} async-done(((bf16[1,80,3584]{2,1,0:T(8,128)(2,1)}), bf16[16,80,3584]{2,1,0:T(8,128)(2,1)}) %all-gather.4.cloned.1.call-update) | async-done | bytes 9175056 | tf_op jit(solution)/shard_map/all_gather | solution.py:62
  187.4 12.1 %copy.55 = bf16[16,80,3584]{2,0,1:T(8,128)(2,1)} copy(bf16[16,80,3584]{2,1,0:T(8,128)(2,1)} %all-gather.4.cloned.1.call-done) | data formatting | bytes 18350080 | tf_op jit(solution)/shard_map/all_gather | solution.py:62
  199.5 13.9 %reshape.74 = bf16[8,2,16,5,3584]{4,1,0,3,2:T(2,128)(2,1)} reshape(bf16[16,80,3584]{2,0,1:T(8,128)(2,1)} %copy.55) | data formatting | bytes 18350080 | tf_op jit(solution)/shard_map/reshape | solution.py:68
  213.4 0.0 copy-start.4
  213.4 9.5 %fusion.23 = f32[8,16,5,256]{3,1,2,0:T(8,128)S(1)} fusion(bf16[2,3584,128]{2,1,0:T(8,128)(2,1)S(1)} %bitcast.121, bf16[2,3584,128]{2,1,0:T(8,128)(2,1)} %bitcast.123, bf16[8,2,16,5,3584]{4,1,0,3,2:T(2,128)(2,1)} %reshape.76), kind=kOutput, calls=%fused_computation.23 | convolution fusion | flops 2356150272 | bytes 13500416 | tf_op jit(solution)/shard_map/dtecf,tfk->deck/dot_general | solution.py:75
  222.9 0.0 copy-start.7
  222.9 5.1 %multiply_convert_fusion.2 = (bf16[8,16,5,128]{3,1,2,0:T(8,128)(2,1)S(1)}, bf16[8,16,5,128]{3,1,2,0:T(8,128)(2,1)S(1)}, bf16[8,16,5,128]{3,1,2,0:T(8,128)(2,1)S(1)}, f32[8,16,5,128]{3,1,2,0:T(8,128)S(1)}) fusion(f32[8,16,5,256]{3,1,2,0:T(8,128)S(1)} %fusion.23, f32[8,16,5]{1,2,0:T(8,128)S(1)} %copy.53, bf16[128,2,3584,1,1]{2,1,0,4,3:T(2,128)(2,1)S(1)} %bitcast.108, ...), kind=kOutput, calls=%fused_computation.39 | convolution fusion | flops 1175715840 | bytes 12487168 | tf_op jit(solution)/shard_map/dtecf,htf->dech/dot_general | solution.py:80
  228.0 3.0 convert_bitcast_fusion
  231.1 11.2 %copy.61 = bf16[8,2,16,5,3584]{4,3,2,1,0:T(8,128)(2,1)} copy(bf16[8,2,16,5,3584]{4,2,3,0,1:T(8,128)(2,1)S(1)} %convert_bitcast_fusion) | data formatting | bytes 18350080 | tf_op jit(solution)/shard_map/convert_element_type | solution.py:116
  242.3 14.9 %convert_element_type.102 = bf16[1280,3584]{1,0:T(8,128)(2,1)} reshape(bf16[8,2,16,5,3584]{4,3,2,1,0:T(8,128)(2,1)} %copy.61) | data formatting | bytes 18350080 | tf_op jit(solution)/shard_map/convert_element_type | solution.py:116
  257.2 0.0 reduce-scatter.2.cloned.1.call-update
  257.2 15.2 %reshape.104 = bf16[7168,5,8,16]{0,2,1,3:T(8,128)(2,1)} reshape(bf16[2,3584,5,8,16]{1,0,3,2,4:T(2,128)(2,1)} %bitcast.107) | data formatting | bytes 18350080 | tf_op jit(solution)/shard_map/dtecf,deck->tfk/dot_general | solution.py:98
  272.4 0.3 fusion.37
  272.7 51.8 %psum.7 = bf16[8,16,5]{1,2,0:T(8,128)(2,1)S(1)} all-reduce(f32[8,16,5]{1,2,0:T(8,128)S(1)} %get-tuple-element.11), channel_id=1, replica_groups=mesh['dp'=8,'expert'=16,'tensor'=2] {'dp','tensor'}, use_global_device_ids=true, to_apply=%region_5.6 | all-reduce | flops 640 | bytes 3840 | tf_op jit(solution)/shard_map/psum | solution.py:104
  324.5 0.7 copy.63
  325.2 8.6 %all-to-all-start.4 = ((bf16[16,1,5]{2,1,0:T(2,128)(2,1)}), bf16[16,1,5]{2,1,0:T(2,128)(2,1)S(1)}, u32[]{:S(2)}, u32[]{:S(2)}) async-start(bf16[16,1,5]{2,1,0:T(2,128)(2,1)} %copy.63), calls=%async_computation.5 | async-start | bytes 16384 | tf_op jit(solution)/shard_map/all_to_all | solution.py:126
  333.8 10.7 %fusion.7 = bf16[7168,256]{1,0:T(8,128)(2,1)S(1)} fusion(bf16[7168,5,8,16]{0,2,1,3:T(8,128)(2,1)} %reshape.104, bf16[8,16,5,128]{3,1,2,0:T(8,128)(2,1)S(1)} %get-tuple-element.8, bf16[8,16,5,128]{3,1,2,0:T(8,128)(2,1)S(1)} %get-tuple-element.7), kind=kOutput, calls=%fused_computation.9 | convolution fusion | flops 2351300608 | bytes 13172736 | tf_op jit(solution)/shard_map/dtecf,deck->tfk/dot_general | solution.py:98
  344.5 2.1 slice_bitcast_fusion
  346.6 15.2 %reshape.105 = bf16[7168,5,8,16]{0,2,1,3:T(8,128)(2,1)} reshape(bf16[2,3584,5,8,16]{1,0,3,2,4:T(2,128)(2,1)} %bitcast.106) | data formatting | bytes 18350080 | tf_op jit(solution)/shard_map/dech,dtecf->htf/dot_general | solution.py:94
  361.8 97.4 %reduce-scatter.2.cloned.1.call-done = bf16[80,3584]{1,0:T(8,128)(2,1)} async-done(((bf16[1280,3584]{1,0:T(8,128)(2,1)}), bf16[80,3584]{1,0:T(8,128)(2,1)}) %reduce-scatter.2.cloned.1.call-update) | async-done | bytes 573456 | tf_op jit(solution)/shard_map/reduce_scatter | solution.py:115
  459.2 2.2 convert_element_type.103
  461.4 0.0 all-to-all-done.4
  461.4 9.5 %all-to-all-start.3 = ((bf16[16,5,3584]{2,1,0:T(8,128)(2,1)}), bf16[16,5,3584]{2,1,0:T(8,128)(2,1)S(1)}, u32[]{:S(2)}, u32[]{:S(2)}) async-start(bf16[16,5,3584]{2,1,0:T(8,128)(2,1)} %convert_element_type.103), calls=%async_computation.4 | async-start | bytes 1835008 | tf_op jit(solution)/shard_map/all_to_all | solution.py:119
  471.0 10.6 %fusion.16 = bf16[1,128,7168]{2,1,0:T(8,128)(2,1)} fusion(bf16[7168,5,8,16]{0,2,1,3:T(8,128)(2,1)} %reshape.105, bf16[8,16,5,128]{3,1,2,0:T(8,128)(2,1)S(1)} %get-tuple-element.10), kind=kOutput, calls=%fused_computation.12 | convolution fusion | flops 1175322624 | bytes 11173888 | tf_op jit(solution)/shard_map/dech,dtecf->htf/dot_general | solution.py:94
  481.6 0.1 copy.98
  481.7 0.1 copy.86
  481.8 0.1 copy.87
  481.9 0.2 fusion.50
  482.1 0.6 convert_element_type.109
  482.7 15.0 %all-to-all-done.3 = bf16[16,5,3584]{2,1,0:T(8,128)(2,1)S(1)} async-done(((bf16[16,5,3584]{2,1,0:T(8,128)(2,1)}), bf16[16,5,3584]{2,1,0:T(8,128)(2,1)S(1)}, u32[]{:S(2)}, u32[]{:S(2)}) %all-to-all-start.3) | async-done | bytes 573472 | tf_op jit(solution)/shard_map/all_to_all | solution.py:119
  497.7 0.9 fusion.19
  (23 shorter events, 0.2 us)
Async XLA Ops:
  7.2 1.0 copy-start
  7.2 75.2 %copy-start.5 = (s32[8,8]{1,0:T(8,128)S(1)}, s32[8,8]{1,0:T(8,128)}, u32[]{:S(2)}) copy-start(s32[8,8]{1,0:T(8,128)} %param.13) | copy-start | bytes 772
  7.2 75.2 %copy-start.8 = (bf16[8,8]{1,0:T(8,128)(2,1)S(1)}, bf16[8,8]{1,0:T(8,128)(2,1)}, u32[]{:S(2)}) copy-start(bf16[8,8]{1,0:T(8,128)(2,1)} %param.12) | copy-start | bytes 388
  7.2 80.3 %copy-start.3 = (bf16[1,128,7168]{2,1,0:T(8,128)(2,1)S(1)}, bf16[1,128,7168]{2,1,0:T(8,128)(2,1)}, u32[]{:S(2)}) copy-start(bf16[1,128,7168]{2,1,0:T(8,128)(2,1)} %param.19) | copy-start | bytes 5505028
  7.2 119.2 %all-gather.6.cloned.1.call-start = ((), (), s32[]{:S(2)}) async-start(), calls=%async_computation.7 | async-start | bytes 9748480 | tf_op jit(solution)/shard_map/all_gather | solution.py:59
  45.1 142.3 %all-gather.4.cloned.1.call-start = ((), (), s32[]{:S(2)}) async-start(), calls=%async_computation.6 | async-start | bytes 9748480 | tf_op jit(solution)/shard_map/all_gather | solution.py:62
  83.3 12.9 %all-to-all-start = ((bf16[16,1,5]{2,1,0:T(2,128)(2,1)}), bf16[16,1,5]{2,1,0:T(2,128)(2,1)S(1)}, u32[]{:S(2)}, u32[]{:S(2)}) async-start(bf16[16,1,5]{2,1,0:T(2,128)(2,1)} %copy.52), calls=%async_computation | async-start | bytes 16384 | tf_op jit(solution)/shard_map/all_to_all | solution.py:56
  87.5 371.7 %reduce-scatter.2.cloned.1.call-start = ((), (), s32[]{:S(2)}) async-start(), calls=%async_computation.8 | async-start | bytes 9748480 | tf_op jit(solution)/shard_map/reduce_scatter | solution.py:115
  199.5 13.9 %copy-start.6 = (bf16[1,7168,128]{2,1,0:T(8,128)(2,1)S(1)}, bf16[1,7168,128]{2,1,0:T(8,128)(2,1)}, u32[]{:S(2)}) copy-start(bf16[1,7168,128]{2,1,0:T(8,128)(2,1)} %param.18) | copy-start | bytes 5505028
  213.4 9.6 %copy-start.2 = (bf16[8,2,16,5,3584]{4,1,0,3,2:T(2,128)(2,1)S(1)}, bf16[8,2,16,5,3584]{4,1,0,3,2:T(2,128)(2,1)}, u32[]{:S(2)}) copy-start(bf16[8,2,16,5,3584]{4,1,0,3,2:T(2,128)(2,1)} %reshape.74) | copy-start | bytes 27525124
  213.4 9.6 %copy-start.4 = (bf16[128,2,3584]{2,1,0:T(2,128)(2,1)S(1)}, bf16[128,2,3584]{2,1,0:T(2,128)(2,1)}, u32[]{:S(2)}) copy-start(bf16[128,2,3584]{2,1,0:T(2,128)(2,1)} %reshape_squeeze.3) | copy-start | bytes 5505028
  222.9 5.1 %copy-start.7 = (bf16[1,7168,128]{2,1,0:T(8,128)(2,1)S(1)}, bf16[1,7168,128]{2,1,0:T(8,128)(2,1)}, u32[]{:S(2)}) copy-start(bf16[1,7168,128]{2,1,0:T(8,128)(2,1)} %param.17) | copy-start | bytes 5505028
  325.2 136.2 %all-to-all-start.4 = ((bf16[16,1,5]{2,1,0:T(2,128)(2,1)}), bf16[16,1,5]{2,1,0:T(2,128)(2,1)S(1)}, u32[]{:S(2)}, u32[]{:S(2)}) async-start(bf16[16,1,5]{2,1,0:T(2,128)(2,1)} %copy.63), calls=%async_computation.5 | async-start | bytes 16384 | tf_op jit(solution)/shard_map/all_to_all | solution.py:126
  346.6 152.1 %copy-start.1 = (bf16[8,3584]{1,0:T(8,128)(2,1)S(1)}, bf16[8,3584]{1,0:T(8,128)(2,1)}, u32[]{:S(2)}) copy-start(bf16[8,3584]{1,0:T(8,128)(2,1)} %param.10) | copy-start | bytes 172036
  461.4 36.3 %all-to-all-start.3 = ((bf16[16,5,3584]{2,1,0:T(8,128)(2,1)}), bf16[16,5,3584]{2,1,0:T(8,128)(2,1)S(1)}, u32[]{:S(2)}, u32[]{:S(2)}) async-start(bf16[16,5,3584]{2,1,0:T(8,128)(2,1)} %convert_element_type.103), calls=%async_computation.4 | async-start | bytes 1835008 | tf_op jit(solution)/shard_map/all_to_all | solution.py:119
Sparse Core Ops, SparseCore 0:
  45.2 76.4 all-gather.5
  124.1 63.2 all-gather.3
  257.3 201.8 reduce-scatter.1
where the time goes:
time: 511 us; the launch traced here: 505 us
  waiting for transfers between devices  154 us (30%)
  blocking collectives  147 us (29%)
  local copies, waits for them, and re-layouts  120 us (23%)
  matrix products  43.7 us (9%)
  starting transfers between devices  22.4 us (4%)
  between operations  14.3 us (3%)
    reduce_scatter x1, waiting for transfers between devices, shards(): lax.psum_scatter(product.astype(jnp.bfloat16), ('dp', 'tensor'), scatter_...  97.4 us
    psum x1, blocking collectives, shards(): route_total = lax.psum(route_part, ('dp', 'tensor'))  51.8 us
    all_to_all x1, blocking collectives, shards(): lax.all_to_all(packed_rows, 'expert', split_axis=0, concat_axis=0, tiled=...  35.1 us
    all_gather x1, waiting for transfers between devices, shards(): lax.all_gather(arrived[1].reshape(1, slots, features), ('dp', 'tensor'),...  35.1 us
    all_to_all x1, blocking collectives, shards(): lax.all_to_all(packed_upstream, 'expert', split_axis=0, concat_axis=0, ti...  30.4 us
    all_gather x1, blocking collectives, shards(): lax.all_gather(arrived[2].reshape(1, slots), ('dp', 'tensor'), axis=0, ti...  29.7 us
    convert_element_type x2, local copies, waits for them, and re-layouts, shards(): product.astype(jnp.bfloat16)  26.1 us
    dot_general x1, local copies, waits for them, and re-layouts, shards(): jnp.einsum('dech,' + layout + '->htf', weighted, rows_back, preferred_ele...  15.2 us
  transfers between devices with their start and end apart: 6, of which 4 were waited for; matrix products, arithmetic and copies ran while one was open for 19% of the time, Pallas kernels for 0%

commit v1 on v0

--- a/solution.py
+++ b/solution.py
@@ -56,8 +56,16 @@
         lax.all_to_all(packed_prob, "expert", split_axis=0, concat_axis=0, tiled=True),
     )
     gathered = (
-        lax.all_gather(
-            arrived[0].reshape(1, slots, features), ("dp", "tensor"), axis=0, tiled=True
+        jnp.concatenate(
+            lax.all_to_all(
+                jnp.stack(
+                    [arrived[0].reshape(1, slots, features)] * lax.axis_size(("dp", "tensor"))
+                ),
+                ("dp", "tensor"),
+                0,
+                0,
+            ),
+            axis=0,
         ),
         lax.all_gather(
             arrived[1].reshape(1, slots, features), ("dp", "tensor"), axis=0, tiled=True

time: 511 us -> 594 us (1.16)
  blocking collectives: 147 us -> 197 us
  starting transfers between devices: 22.4 us -> 38.3 us
  local copies, waits for them, and re-layouts: 120 us -> 127 us
  waiting for transfers between devices: 154 us -> 161 us
    all_gather x1, blocking collectives: 29.7 us -> 141 us  [shards(): lax.all_gather(arrived[2].reshape(1, slots), ('dp', 'tensor'), axis=0, ti...]
    all_to_all x2 -> x0, blocking collectives: 65.5 us -> none  [the longest x1 35.1 us: shards(): lax.all_to_all(packed_rows, 'expert', split_axis=0, concat_axis=0, tiled=...]
    all_to_all x0 -> x3, waiting for transfers between devices: none -> 43.9 us  [the longest x1 26.4 us: shards(): lax.all_to_all(packed_upstream, 'expert', split_axis=0, concat_axis=0, ti...]
    all_gather x1, waiting for transfers between devices: 35.1 us -> 0.01 us  [shards(): lax.all_gather(arrived[1].reshape(1, slots, features), ('dp', 'tensor'),...]
    another operation x0 -> x3, local copies, waits for them, and re-layouts: none -> 18.3 us  [the longest x1 13.6 us: shards(): gathered[0].reshape(dp_size, tensor_size, experts, capacity, features)]
    all_to_all x0 -> x3, starting transfers between devices: none -> 15.1 us  [the longest x1 5.94 us: shards(): lax.all_to_all(jnp.stack([arrived[0].reshape(1, slots, features)] * lax.a...]
    reshape x2 -> x0, local copies, waits for them, and re-layouts: 14.8 us -> none  [the longest x1 13.8 us: shards(): gathered[0].reshape(dp_size, tensor_size, experts, capacity, features)]
    all_to_all x0 -> x1, local copies, waits for them, and re-layouts: none -> 12.2 us  [shards(): lax.all_to_all(jnp.stack([arrived[0].reshape(1, slots, features)] * lax.a...]
  transfers between devices with their start and end apart: 6 -> 8, of which waited for: 4 -> 5; matrix products, arithmetic and copies ran while one was open for 19% -> 17% of each run, Pallas kernels for 0% -> 0%
where the time goes in v1:
time: 594 us; the launch traced here: 587 us
  blocking collectives  197 us (33%)
  waiting for transfers between devices  161 us (27%)
  local copies, waits for them, and re-layouts  127 us (21%)
  matrix products  44.8 us (8%)
  starting transfers between devices  38.3 us (6%)
  between operations  14.5 us (2%)
    all_gather x1, blocking collectives, shards(): lax.all_gather(arrived[2].reshape(1, slots), ('dp', 'tensor'), axis=0, ti...  141 us
    reduce_scatter x1, waiting for transfers between devices, shards(): lax.psum_scatter(product.astype(jnp.bfloat16), ('dp', 'tensor'), scatter_...  94.8 us
    psum x1, blocking collectives, shards(): route_total = lax.psum(route_part, ('dp', 'tensor'))  56.3 us
    all_to_all x1, waiting for transfers between devices, shards(): lax.all_to_all(packed_upstream, 'expert', split_axis=0, concat_axis=0, ti...  26.4 us
    convert_element_type x2, local copies, waits for them, and re-layouts, shards(): product.astype(jnp.bfloat16)  26.1 us
    all_to_all x1, waiting for transfers between devices, shards(): lax.all_to_all(packed_rows, 'expert', split_axis=0, concat_axis=0, tiled=...  17.5 us
    dot_general x1, local copies, waits for them, and re-layouts, shards(): jnp.einsum(layout + ',deck->tfk', rows_in, grad_inner, preferred_element_...  15.3 us
    dot_general x1, local copies, waits for them, and re-layouts, shards(): jnp.einsum('dech,' + layout + '->htf', weighted, rows_back, preferred_ele...  15.2 us
  transfers between devices with their start and end apart: 8, of which 5 were waited for; matrix products, arithmetic and copies ran while one was open for 17% of the time, Pallas kernels for 0%

profile of v1, /device:TPU:35, one launch (start us, length us, event | category | flops | bytes accessed | tf_op | source)
XLA Modules:
  0.0 587.1 jit_solution(2691968681973451976)
XLA Ops:
  7.2 0.0 copy-start
  7.2 0.8 convert_reduce_fusion
  8.0 0.9 fusion.51
  8.9 0.7 copy.51
  9.6 10.0 %all-to-all-start = ((bf16[16,1,5]{2,1,0:T(2,128)(2,1)}), bf16[16,1,5]{2,1,0:T(2,128)(2,1)S(1)}, u32[]{:S(2)}, u32[]{:S(2)}) async-start(bf16[16,1,5]{2,1,0:T(2,128)(2,1)} %copy.51), calls=%async_computation | async-start | bytes 16384 | tf_op jit(solution)/shard_map/all_to_all | solution.py:56
  19.7 0.3 convolution_convert_fusion
  20.0 1.3 copy.57
  21.3 7.1 %all-to-all-done = bf16[16,1,5]{2,1,0:T(2,128)(2,1)S(1)} async-done(((bf16[16,1,5]{2,1,0:T(2,128)(2,1)}), bf16[16,1,5]{2,1,0:T(2,128)(2,1)S(1)}, u32[]{:S(2)}, u32[]{:S(2)}) %all-to-all-start) | async-done | bytes 192 | tf_op jit(solution)/shard_map/all_to_all | solution.py:56
  28.4 3.6 all-to-all-start.2
  32.0 0.7 convert_element_type.94
  32.7 0.9 fusion.41
  33.6 1.0 fusion.34
  34.7 0.8 divide_subtract_fusion
  35.4 0.8 convolution_bitcast_fusion.2
  36.3 1.2 convolution_convert_fusion.1
  37.4 1.3 copy.53
  38.7 17.5 %all-to-all-done.2 = bf16[16,5,3584]{2,1,0:T(8,128)(2,1)S(1)} async-done(((bf16[16,5,3584]{2,1,0:T(8,128)(2,1)}), bf16[16,5,3584]{2,1,0:T(8,128)(2,1)S(1)}, u32[]{:S(2)}, u32[]{:S(2)}) %all-to-all-start.2) | async-done | bytes 573472 | tf_op jit(solution)/shard_map/all_to_all | solution.py:54
  56.2 5.5 all-to-all-start.1
  61.7 0.2 stack_reshape.2
  62.0 26.4 %all-to-all-done.1 = bf16[16,5,3584]{2,1,0:T(8,128)(2,1)S(1)} async-done(((bf16[16,5,3584]{2,1,0:T(8,128)(2,1)}), bf16[16,5,3584]{2,1,0:T(8,128)(2,1)S(1)}, u32[]{:S(2)}, u32[]{:S(2)}) %all-to-all-start.1) | async-done | bytes 573472 | tf_op jit(solution)/shard_map/all_to_all | solution.py:55
  88.4 4.5 stack.3
  92.9 5.9 %all-to-all-start.3 = ((bf16[16,1,80,3584]{3,2,1,0:T(8,128)(2,1)}), bf16[16,1,80,3584]{3,2,1,0:T(8,128)(2,1)}, u32[]{:S(2)}, u32[]{:S(2)}) async-start(bf16[16,1,80,3584]{3,2,1,0:T(8,128)(2,1)} %stack.3), calls=%async_computation.3 | async-start | bytes 18350080 | tf_op jit(solution)/shard_map/all_to_all | solution.py:60
  98.8 0.0 all-gather.3.cloned.1.call-start
  98.9 1.0 reshape.71
  99.9 0.0 all-gather.3.cloned.1.call-update
  99.9 0.0 reduce-scatter.2.cloned.1.call-start
  100.0 4.6 reshape_squeeze.3
  104.6 0.1 reshape.74
  104.7 140.8 %all-gather = bf16[16,1,80]{2,1,0:T(2,128)(2,1)S(1)} all-gather(bf16[1,1,80]{2,1,0:T(2,128)(2,1)S(1)} %reshape.74), channel_id=1, replica_groups=mesh['dp'=8,'expert'=16,'tensor'=2] {'dp','tensor'}, dimensions={0}, use_global_device_ids=true | all-gather | bytes 2720 | tf_op jit(solution)/shard_map/all_gather | solution.py:73
  245.6 0.1 reshape.70
  245.7 0.1 copy.52
  245.8 0.0 all-to-all-done.3
  245.8 12.2 %copy.58 = bf16[16,1,80,3584]{3,0,2,1:T(8,128)(2,1)} copy(bf16[16,1,80,3584]{3,2,1,0:T(8,128)(2,1)} %all-to-all-done.3) | data formatting | bytes 18350080 | tf_op jit(solution)/shard_map/all_to_all | solution.py:60
  258.0 13.6 %reshape_reshape.3 = bf16[8,2,16,5,3584]{4,1,0,3,2:T(2,128)(2,1)} reshape(bf16[16,1,80,3584]{3,0,2,1:T(8,128)(2,1)} %copy.58) | data formatting | bytes 18350080 | tf_op jit(solution)/shard_map/reshape;reshape | solution.py:75
  271.6 12.1 %copy.54 = bf16[16,80,3584]{2,0,1:T(8,128)(2,1)} copy(bf16[16,80,3584]{2,1,0:T(8,128)(2,1)} %all-gather.3.cloned.1.call-done) | data formatting | bytes 18350080 | tf_op jit(solution)/shard_map/all_gather | solution.py:70
  283.6 13.7 %reshape.72 = bf16[8,2,16,5,3584]{4,1,0,3,2:T(2,128)(2,1)} reshape(bf16[16,80,3584]{2,0,1:T(8,128)(2,1)} %copy.54) | data formatting | bytes 18350080 | tf_op jit(solution)/shard_map/reshape | solution.py:76
  297.4 10.0 %fusion.23 = f32[8,16,5,256]{3,1,2,0:T(8,128)S(1)} fusion(bf16[2,3584,128]{2,1,0:T(8,128)(2,1)} %bitcast.123, bf16[2,3584,128]{2,1,0:T(8,128)(2,1)} %bitcast.125, bf16[8,2,16,5,3584]{4,1,0,3,2:T(2,128)(2,1)} %reshape_reshape.3), kind=kOutput, calls=%fused_computation.23 | convolution fusion | flops 2356150272 | bytes 13500416 | tf_op jit(solution)/shard_map/dtecf,tfk->deck/dot_general | solution.py:83
  307.4 0.0 copy-start.4
  307.4 0.0 copy-start.5
  307.4 5.1 multiply_convert_fusion.2
  312.5 3.0 convert_bitcast_fusion
  315.5 11.2 %copy.60 = bf16[8,2,16,5,3584]{4,3,2,1,0:T(8,128)(2,1)} copy(bf16[8,2,16,5,3584]{4,2,3,0,1:T(8,128)(2,1)S(1)} %convert_bitcast_fusion) | data formatting | bytes 18350080 | tf_op jit(solution)/shard_map/convert_element_type | solution.py:124
  326.7 14.9 %convert_element_type.102 = bf16[1280,3584]{1,0:T(8,128)(2,1)} reshape(bf16[8,2,16,5,3584]{4,3,2,1,0:T(8,128)(2,1)} %copy.60) | data formatting | bytes 18350080 | tf_op jit(solution)/shard_map/convert_element_type | solution.py:124
  341.6 0.0 reduce-scatter.2.cloned.1.call-update
  341.7 15.3 %reshape.100 = bf16[7168,5,8,16]{0,2,1,3:T(8,128)(2,1)} reshape(bf16[2,3584,5,8,16]{1,0,3,2,4:T(2,128)(2,1)} %bitcast.109) | data formatting | bytes 18350080 | tf_op jit(solution)/shard_map/dtecf,deck->tfk/dot_general | solution.py:106
  356.9 0.3 fusion.37
  357.2 56.3 %psum.7 = bf16[8,16,5]{1,2,0:T(8,128)(2,1)S(1)} all-reduce(f32[8,16,5]{1,2,0:T(8,128)S(1)} %get-tuple-element.11), channel_id=1, replica_groups=mesh['dp'=8,'expert'=16,'tensor'=2] {'dp','tensor'}, use_global_device_ids=true, to_apply=%region_5.6 | all-reduce | flops 640 | bytes 3840 | tf_op jit(solution)/shard_map/psum | solution.py:112
  413.5 0.7 copy.62
  414.2 3.5 all-to-all-start.5
  417.7 10.7 %fusion.7 = bf16[7168,256]{1,0:T(8,128)(2,1)S(1)} fusion(bf16[7168,5,8,16]{0,2,1,3:T(8,128)(2,1)} %reshape.100, bf16[8,16,5,128]{3,1,2,0:T(8,128)(2,1)S(1)} %get-tuple-element.8, bf16[8,16,5,128]{3,1,2,0:T(8,128)(2,1)S(1)} %get-tuple-element.7), kind=kOutput, calls=%fused_computation.9 | convolution fusion | flops 2351300608 | bytes 13172736 | tf_op jit(solution)/shard_map/dtecf,deck->tfk/dot_general | solution.py:106
  428.5 2.1 slice_bitcast_fusion
  430.5 15.2 %reshape.101 = bf16[7168,5,8,16]{0,2,1,3:T(8,128)(2,1)} reshape(bf16[2,3584,5,8,16]{1,0,3,2,4:T(2,128)(2,1)} %bitcast.108) | data formatting | bytes 18350080 | tf_op jit(solution)/shard_map/dech,dtecf->htf/dot_general | solution.py:102
  445.8 94.8 %reduce-scatter.2.cloned.1.call-done = bf16[80,3584]{1,0:T(8,128)(2,1)} async-done(((bf16[1280,3584]{1,0:T(8,128)(2,1)}), bf16[80,3584]{1,0:T(8,128)(2,1)}) %reduce-scatter.2.cloned.1.call-update) | async-done | bytes 573456 | tf_op jit(solution)/shard_map/reduce_scatter | solution.py:123
  540.6 2.2 convert_element_type.103
  542.8 0.0 all-to-all-done.5
  542.8 9.5 %all-to-all-start.4 = ((bf16[16,5,3584]{2,1,0:T(8,128)(2,1)}), bf16[16,5,3584]{2,1,0:T(8,128)(2,1)S(1)}, u32[]{:S(2)}, u32[]{:S(2)}) async-start(bf16[16,5,3584]{2,1,0:T(8,128)(2,1)} %convert_element_type.103), calls=%async_computation.5 | async-start | bytes 1835008 | tf_op jit(solution)/shard_map/all_to_all | solution.py:127
  552.3 10.6 %fusion.16 = bf16[1,128,7168]{2,1,0:T(8,128)(2,1)} fusion(bf16[7168,5,8,16]{0,2,1,3:T(8,128)(2,1)} %reshape.101, bf16[8,16,5,128]{3,1,2,0:T(8,128)(2,1)S(1)} %get-tuple-element.10), kind=kOutput, calls=%fused_computation.12 | convolution fusion | flops 1175322624 | bytes 11173888 | tf_op jit(solution)/shard_map/dech,dtecf->htf/dot_general | solution.py:102
  562.9 0.1 copy.97
  563.1 0.1 copy.85
  563.1 0.1 copy.86
  563.2 0.2 fusion.50
  563.4 0.6 convert_element_type.109
  564.0 15.0 %all-to-all-done.4 = bf16[16,5,3584]{2,1,0:T(8,128)(2,1)S(1)} async-done(((bf16[16,5,3584]{2,1,0:T(8,128)(2,1)}), bf16[16,5,3584]{2,1,0:T(8,128)(2,1)S(1)}, u32[]{:S(2)}, u32[]{:S(2)}) %all-to-all-start.4) | async-done | bytes 573472 | tf_op jit(solution)/shard_map/all_to_all | solution.py:127
  579.1 0.9 fusion.19
  (19 shorter events, 0.2 us)
Async XLA Ops:
  7.2 12.5 %copy-start = (bf16[8,3584]{1,0:T(8,128)(2,1)S(1)}, bf16[8,3584]{1,0:T(8,128)(2,1)}, u32[]{:S(2)}) copy-start(bf16[8,3584]{1,0:T(8,128)(2,1)} %param.10) | copy-start | bytes 172036
  9.6 18.8 %all-to-all-start = ((bf16[16,1,5]{2,1,0:T(2,128)(2,1)}), bf16[16,1,5]{2,1,0:T(2,128)(2,1)S(1)}, u32[]{:S(2)}, u32[]{:S(2)}) async-start(bf16[16,1,5]{2,1,0:T(2,128)(2,1)} %copy.51), calls=%async_computation | async-start | bytes 16384 | tf_op jit(solution)/shard_map/all_to_all | solution.py:56
  28.4 27.8 %all-to-all-start.2 = ((bf16[16,5,3584]{2,1,0:T(8,128)(2,1)}), bf16[16,5,3584]{2,1,0:T(8,128)(2,1)S(1)}, u32[]{:S(2)}, u32[]{:S(2)}) async-start(bf16[16,5,3584]{2,1,0:T(8,128)(2,1)} %copy.57), calls=%async_computation.2 | async-start | bytes 1835008 | tf_op jit(solution)/shard_map/all_to_all | solution.py:54
  56.2 32.2 %all-to-all-start.1 = ((bf16[16,5,3584]{2,1,0:T(8,128)(2,1)}), bf16[16,5,3584]{2,1,0:T(8,128)(2,1)S(1)}, u32[]{:S(2)}, u32[]{:S(2)}) async-start(bf16[16,5,3584]{2,1,0:T(8,128)(2,1)} %copy.53), calls=%async_computation.1 | async-start | bytes 1835008 | tf_op jit(solution)/shard_map/all_to_all | solution.py:55
  92.9 152.9 %all-to-all-start.3 = ((bf16[16,1,80,3584]{3,2,1,0:T(8,128)(2,1)}), bf16[16,1,80,3584]{3,2,1,0:T(8,128)(2,1)}, u32[]{:S(2)}, u32[]{:S(2)}) async-start(bf16[16,1,80,3584]{3,2,1,0:T(8,128)(2,1)} %stack.3), calls=%async_computation.3 | async-start | bytes 18350080 | tf_op jit(solution)/shard_map/all_to_all | solution.py:60
  98.8 172.7 %all-gather.3.cloned.1.call-start = ((), (), s32[]{:S(2)}) async-start(), calls=%async_computation.7 | async-start | bytes 9748480 | tf_op jit(solution)/shard_map/all_gather | solution.py:70
  99.9 440.6 %reduce-scatter.2.cloned.1.call-start = ((), (), s32[]{:S(2)}) async-start(), calls=%async_computation.8 | async-start | bytes 9748480 | tf_op jit(solution)/shard_map/reduce_scatter | solution.py:123
  297.4 10.0 %copy-start.2 = (bf16[8,2,16,5,3584]{4,1,0,3,2:T(2,128)(2,1)S(1)}, bf16[8,2,16,5,3584]{4,1,0,3,2:T(2,128)(2,1)}, u32[]{:S(2)}) copy-start(bf16[8,2,16,5,3584]{4,1,0,3,2:T(2,128)(2,1)} %reshape.72) | copy-start | bytes 27525124
  307.4 5.1 copy-start.4
  307.4 5.1 copy-start.5
  414.2 128.6 %all-to-all-start.5 = ((bf16[16,1,5]{2,1,0:T(2,128)(2,1)}), bf16[16,1,5]{2,1,0:T(2,128)(2,1)S(1)}, u32[]{:S(2)}, u32[]{:S(2)}) async-start(bf16[16,1,5]{2,1,0:T(2,128)(2,1)} %copy.62), calls=%async_computation.6 | async-start | bytes 16384 | tf_op jit(solution)/shard_map/all_to_all | solution.py:134
  430.5 149.5 %copy-start.1 = (bf16[8,3584]{1,0:T(8,128)(2,1)S(1)}, bf16[8,3584]{1,0:T(8,128)(2,1)}, u32[]{:S(2)}) copy-start(bf16[8,3584]{1,0:T(8,128)(2,1)} %param.10) | copy-start | bytes 172036
  445.7 117.5 %copy-start.3 = (s32[8,8]{1,0:T(8,128)S(1)}, s32[8,8]{1,0:T(8,128)}, u32[]{:S(2)}) copy-start(s32[8,8]{1,0:T(8,128)} %param.13) | copy-start | bytes 772
  542.8 36.3 %all-to-all-start.4 = ((bf16[16,5,3584]{2,1,0:T(8,128)(2,1)}), bf16[16,5,3584]{2,1,0:T(8,128)(2,1)S(1)}, u32[]{:S(2)}, u32[]{:S(2)}) async-start(bf16[16,5,3584]{2,1,0:T(8,128)(2,1)} %convert_element_type.103), calls=%async_computation.5 | async-start | bytes 1835008 | tf_op jit(solution)/shard_map/all_to_all | solution.py:127
Sparse Core Ops, SparseCore 0:
  102.0 147.7 all-gather.2
  341.8 198.7 reduce-scatter.1
